TPU v7x, 512 devices: a whole 4x4x16 slice. The times are simulated.
512 devices in a mesh: mpo: 8 (over y, core), sec: 64 (over x, z).
Axes of the slice: x: 4, y: 4, z: 16, core: 2. Of those that a mesh axis runs over, the one named last changes fastest.
Arguments:
- theta: bfloat16 [16, 1024, 1024], P(None, 'sec'), may hold values from -6 to 6
- env_left: bfloat16 [24, 16384, 1024], P('mpo', 'sec'), may hold values from -0.1875 to 0.1875
- env_right: bfloat16 [24, 16384, 1024], P('mpo', 'sec'), may hold values from -0.0390625 to 0.0390625
- mpo_core: float32 [24, 24], replicated, may hold values from -1.25 to 1.25
- sector_sizes: int32 [16], replicated, may hold values from 1 to 1024, 12288 in all
Outputs:
- applied: bfloat16 [1024, 16384], P('mpo', 'sec')
Inputs may be any that keep to these rules, and one draw needn't show every extreme that they name: `sector_sizes`: one sector has exactly 1024 states in use; the sizes sum to 12288.
All inputs are finite; a program needn't handle non-finite values.
Results may differ from a plain program's by a relative error of at most 0.0058.
Values may be sent and summed in bfloat16 or wider, within the bound.
No kernel may reach another device: no remote copies, remote signals or barrier semaphores. Data moves between devices by JAX's collectives and lax.ppermute only.
A program may use at most 64 MiB of HBM per device.

v0:
```python
import jax
import jax.numpy as jnp
from jax import lax
from jax.sharding import PartitionSpec as P

G = 4


def swapped(array, axis, stride):
    return lax.ppermute(array, axis, [(i, i ^ 1 << stride) for i in range(lax.axis_size(axis))])


def on_device(theta, env_left, env_right, mpo_core, sector_sizes):
    sectors = theta.shape[0]
    rows_local = theta.shape[1]
    width = theta.shape[2]
    local_w = env_left.shape[0]
    slab = env_left.shape[1]
    sec_place = lax.axis_index("sec")
    sector = sec_place // G
    block_pos = sec_place % G
    live_size = jnp.sum(jnp.where(jnp.arange(sectors, dtype=jnp.int32) == sector, sector_sizes, 0))
    bit_count = G.bit_length() - 1
    spread = jnp.broadcast_to(theta[:, None], (sectors, G, rows_local, width))
    spread = spread.reshape(sectors * G, rows_local, width)
    sector_block = lax.all_to_all(spread, "sec", split_axis=0, concat_axis=1, tiled=True)[0]
    positions = jnp.arange(width, dtype=jnp.int32)
    keep_row = positions < live_size
    sector_block = jnp.where(
        keep_row[:, None] & keep_row[None, :], sector_block, jnp.zeros_like(sector_block)
    )
    product = jnp.einsum(
        "akm,mn->akn", env_left, sector_block, preferred_element_type=jnp.float32
    ).astype(jnp.bfloat16)
    own_start = lax.axis_index("mpo") * local_w
    core_cols = lax.dynamic_slice_in_dim(mpo_core, own_start, local_w, 1)
    mixed = jnp.einsum(
        "ab,akn->bkn",
        core_cols,
        lax.all_gather(product, "mpo", axis=0, tiled=True).astype(jnp.float32),
        precision=lax.Precision.HIGHEST,
    ).astype(jnp.bfloat16)
    for bit_index in range(bit_count):
        partner = swapped(mixed, "sec", bit_index)
        upper_half = sec_place >> bit_index & 1 == 1
        mixed = jnp.where(
            upper_half, jnp.concatenate([partner, mixed], 1), jnp.concatenate([mixed, partner], 1)
        )
    col_keep = block_pos * slab + jnp.arange(slab, dtype=jnp.int32) < live_size
    sector_term = jnp.einsum("bil,bjl->ij", mixed, env_right, preferred_element_type=jnp.float32)
    row_keep = (
        jnp.arange(lax.axis_size("mpo") * (width // lax.axis_size("mpo")), dtype=jnp.int32)
        < live_size
    )
    result = lax.psum_scatter(
        jnp.where(row_keep[:, None] & col_keep[None, :], sector_term, jnp.zeros_like(sector_term)),
        "mpo",
        scatter_dimension=0,
        tiled=True,
    )
    return result.astype(jnp.bfloat16)


def solution(mesh):
    return jax.shard_map(
        on_device,
        mesh=mesh,
        in_specs=(P(None, "sec", None), P("mpo", "sec", None), P("mpo", "sec", None), P(), P()),
        out_specs=P("mpo", "sec"),
        check_vma=False,
    )
```

profile of v0, /device:TPU:2, one launch (start us, length us, event | category | flops | bytes accessed | tf_op | source)
XLA Modules:
  0.0 477.4 jit_solution(1534336615428155424)
XLA Ops:
  6.5 0.0 copy-start
  6.5 2.8 broadcast_in_dim.11
  9.3 18.8 %all-to-all-start = ((bf16[64,16,1024]{2,1,0:T(8,128)(2,1)}), bf16[64,16,1024]{2,1,0:T(8,128)(2,1)}, u32[]{:S(2)}, u32[]{:S(2)}) async-start(bf16[64,16,1024]{2,1,0:T(8,128)(2,1)} %bitcast.21), calls=%async_computation | async-start | bytes 4194304 | tf_op jit(solution)/shard_map/all_to_all | solution.py:26
  28.1 0.0 all-gather.2.cloned.1.call-start
  28.2 0.0 copy-done.7
  28.2 0.6 fusion.27
  28.8 0.6 iota_compare_fusion
  29.5 95.7 %all-to-all-done = bf16[64,16,1024]{2,1,0:T(8,128)(2,1)} async-done(((bf16[64,16,1024]{2,1,0:T(8,128)(2,1)}), bf16[64,16,1024]{2,1,0:T(8,128)(2,1)}, u32[]{:S(2)}, u32[]{:S(2)}) %all-to-all-start) | async-done | bytes 2097184 | tf_op jit(solution)/shard_map/all_to_all | solution.py:26
  125.2 4.9 %fusion.15 = bf16[3,256,1024]{2,1,0:T(8,128)(2,1)} fusion(bf16[3,256,1024]{2,1,0:T(8,128)(2,1)S(1)} %copy-done, bf16[1024,1024]{1,0:T(8,128)(2,1)} %bitcast.2, pred[1024]{0:T(1024)(128)(4,1)S(1)} %iota_compare_fusion), kind=kOutput, calls=%fused_computation.13 | convolution fusion | flops 1613496320 | bytes 5243904 | tf_op jit(solution)/shard_map/akm,mn->akn/dot_general | solution.py:32
  130.1 0.0 all-gather.2.cloned.1.call-update
  130.1 0.0 reduce-scatter.2.cloned.1.call-start
  130.2 69.3 %all-gather.2.cloned.1.call-done = bf16[24,256,1024]{2,1,0:T(8,128)(2,1)} async-done(((bf16[3,256,1024]{2,1,0:T(8,128)(2,1)}), bf16[24,256,1024]{2,1,0:T(8,128)(2,1)}) %all-gather.2.cloned.1.call-update) | async-done | bytes 12582928 | tf_op jit(solution)/shard_map/all_gather | solution.py:40
  199.5 17.3 %fusion.9 = bf16[3,256,1024]{2,0,1:T(4,128)(2,1)S(1)} fusion(bf16[24,256,1024]{2,1,0:T(8,128)(2,1)} %all-gather.2.cloned.1.call-done, f32[24,24]{1,0:T(8,128)S(1)} %copy-done.5, s32[]{:T(128)S(6)} %select_n.47), kind=kOutput, calls=%fused_computation.11 | convolution fusion | flops 227278848 | bytes 14158084 | tf_op jit(solution)/shard_map/ab,akn->bkn/dot_general | solution.py:37
  216.8 1.3 copy-done.3
  218.1 1.8 copy.10
  219.8 3.6 collective-permute-start
  223.5 35.0 %collective-permute-done = bf16[3,256,1024]{2,1,0:T(8,128)(2,1)S(1)} collective-permute-done((bf16[3,256,1024]{2,1,0:T(8,128)(2,1)}, bf16[3,256,1024]{2,1,0:T(8,128)(2,1)S(1)}, u32[]{:S(2)}, u32[]{:S(2)}) %collective-permute-start) | collective-permute-done | bytes 1572896 | tf_op jit(solution)/shard_map/ppermute | solution.py:10
  258.5 1.4 copy.11
  259.9 4.7 maximum_select_fusion.1
  264.5 1.9 copy-done.1
  266.5 2.9 copy.13
  269.4 4.4 collective-permute-start.1
  273.9 0.0 copy-start.2
  273.9 0.8 add_compare_fusion
  274.7 134.6 %collective-permute-done.1 = bf16[3,512,1024]{2,1,0:T(8,128)(2,1)} collective-permute-done((bf16[3,512,1024]{2,1,0:T(8,128)(2,1)}, bf16[3,512,1024]{2,1,0:T(8,128)(2,1)}, u32[]{:S(2)}, u32[]{:S(2)}) %collective-permute-start.1) | collective-permute-done | bytes 3145760 | tf_op jit(solution)/shard_map/ppermute | solution.py:10
  409.3 4.6 copy.14
  413.9 0.0 copy-start.6
  413.9 9.3 %maximum_select_fusion = bf16[3,1024,1024]{2,0,1:T(4,128)(2,1)S(1)} fusion(bf16[3,512,1024]{2,0,1:T(4,128)(2,1)S(1)} %copy-done.2, bf16[3,512,1024]{2,0,1:T(4,128)(2,1)S(1)} %copy.14, pred[]{:T(512)S(6)} %eq.16), kind=kLoop, calls=%fused_computation.2 | loop fusion | flops 9437184 | bytes 12582913 | tf_op jit(solution)/shard_map/jit(_where)/select_n | solution.py:46
  423.3 5.2 %fusion.21 = f32[1024,256]{1,0:T(8,128)} fusion(bf16[3,256,1024]{2,1,0:T(8,128)(2,1)S(1)} %copy-done.6, bf16[3,1024,1024]{2,0,1:T(4,128)(2,1)S(1)} %maximum_select_fusion, pred[256]{0:T(512)(128)(4,1)S(1)} %add_compare_fusion, pred[1024]{0:T(1024)(128)(4,1)S(1)} %iota_compare_fusion), kind=kOutput, calls=%fused_computation.15 | convolution fusion | flops 1611137024 | bytes 8914176 | tf_op jit(solution)/shard_map/bil,bjl->ij/dot_general | solution.py:50
  428.5 0.0 reduce-scatter.2.cloned.1.call-update
  428.5 40.5 %reduce-scatter.2.cloned.1.call-done = f32[128,256]{1,0:T(8,128)} async-done(((f32[1024,256]{1,0:T(8,128)}), f32[128,256]{1,0:T(8,128)}) %reduce-scatter.2.cloned.1.call-update) | async-done | bytes 131088 | tf_op jit(solution)/shard_map/reduce_scatter | solution.py:55
  469.0 1.5 convert_element_type.16
  (10 shorter events, 0.0 us)
Async XLA Ops:
  6.5 118.7 %copy-start = (bf16[3,256,1024]{2,1,0:T(8,128)(2,1)S(1)}, bf16[3,256,1024]{2,1,0:T(8,128)(2,1)}, u32[]{:S(2)}) copy-start(bf16[3,256,1024]{2,1,0:T(8,128)(2,1)} %param.6) | copy-start | bytes 4718596
  6.5 21.7 %copy-start.7 = (s32[16]{0:T(128)S(1)}, s32[16]{0:T(128)}, u32[]{:S(2)}) copy-start(s32[16]{0:T(128)} %param.9) | copy-start | bytes 196
  9.3 115.9 %all-to-all-start = ((bf16[64,16,1024]{2,1,0:T(8,128)(2,1)}), bf16[64,16,1024]{2,1,0:T(8,128)(2,1)}, u32[]{:S(2)}, u32[]{:S(2)}) async-start(bf16[64,16,1024]{2,1,0:T(8,128)(2,1)} %bitcast.21), calls=%async_computation | async-start | bytes 4194304 | tf_op jit(solution)/shard_map/all_to_all | solution.py:26
  28.1 171.4 %all-gather.2.cloned.1.call-start = ((), (), s32[]{:S(2)}) async-start(), calls=%async_computation.2 | async-start | bytes 14155776 | tf_op jit(solution)/shard_map/all_gather | solution.py:40
  125.2 74.3 %copy-start.5 = (f32[24,24]{1,0:T(8,128)S(1)}, f32[24,24]{1,0:T(8,128)}, u32[]{:S(2)}) copy-start(f32[24,24]{1,0:T(8,128)} %param.8) | copy-start | bytes 6916
  130.1 338.9 %reduce-scatter.2.cloned.1.call-start = ((), (), s32[]{:S(2)}) async-start(), calls=%async_computation.3 | async-start | bytes 1179648 | tf_op jit(solution)/shard_map/reduce_scatter | solution.py:55
  216.8 1.3 copy-start.3
  219.8 38.6 %collective-permute-start = (bf16[3,256,1024]{2,1,0:T(8,128)(2,1)}, bf16[3,256,1024]{2,1,0:T(8,128)(2,1)S(1)}, u32[]{:S(2)}, u32[]{:S(2)}) collective-permute-start(bf16[3,256,1024]{2,1,0:T(8,128)(2,1)} %copy.10), channel_id=1, source_target_pairs={{0,1},{1,0},{2,3},{3,2},{4,5},{5,4},{6,7},{7,6},{8,9},{9,8},{10,11... | collective-permute-start | bytes 4718600 | tf_op jit(solution)/shard_map/ppermute | solution.py:10
  223.5 36.4 %copy-start.4 = (bf16[3,256,1024]{2,0,1:T(4,128)(2,1)S(1)}, bf16[3,256,1024]{2,0,1:T(4,128)(2,1)}, u32[]{:S(2)}) copy-start(bf16[3,256,1024]{2,0,1:T(4,128)(2,1)} %copy-done.3) | copy-start | bytes 4718596
  264.5 2.0 copy-start.1
  269.4 139.9 %collective-permute-start.1 = (bf16[3,512,1024]{2,1,0:T(8,128)(2,1)}, bf16[3,512,1024]{2,1,0:T(8,128)(2,1)}, u32[]{:S(2)}, u32[]{:S(2)}) collective-permute-start(bf16[3,512,1024]{2,1,0:T(8,128)(2,1)} %copy.13), channel_id=1, source_target_pairs={{0,2},{1,3},{2,0},{3,1},{4,6},{5,7},{6,4},{7,5},{8,10},{9,11},{10,... | collective-permute-start | bytes 9437192 | tf_op jit(solution)/shard_map/ppermute | solution.py:10
  273.9 140.0 %copy-start.2 = (bf16[3,512,1024]{2,0,1:T(4,128)(2,1)S(1)}, bf16[3,512,1024]{2,0,1:T(4,128)(2,1)}, u32[]{:S(2)}) copy-start(bf16[3,512,1024]{2,0,1:T(4,128)(2,1)} %copy-done.1) | copy-start | bytes 9437188
  413.9 9.3 %copy-start.6 = (bf16[3,256,1024]{2,1,0:T(8,128)(2,1)S(1)}, bf16[3,256,1024]{2,1,0:T(8,128)(2,1)}, u32[]{:S(2)}) copy-start(bf16[3,256,1024]{2,1,0:T(8,128)(2,1)} %param.7) | copy-start | bytes 4718596
Sparse Core Ops, SparseCore 0:
  130.3 69.1 all-gather.1
  428.7 40.3 reduce-scatter.1
where the time goes:
time: 478 us; the launch traced here: 477 us
  waiting for transfers between devices  375 us (78%)
  matrix products  27.4 us (6%)
  starting transfers between devices  27 us (6%)
  other arithmetic  17.6 us (4%)
  local copies, waits for them, and re-layouts  16.7 us (3%)
  between operations  13.6 us (3%)
    ppermute x2, waiting for transfers between devices, swapped(): lax.ppermute(array, axis, [(i, i ^ 1 << stride) for i in range(lax.axis_s...  170 us
    all_to_all x1, waiting for transfers between devices, on_device(): lax.all_to_all(spread, 'sec', split_axis=0, concat_axis=1, tiled=True)[0]  95.7 us
    all_gather x1, waiting for transfers between devices, on_device(): lax.all_gather(product, 'mpo', axis=0, tiled=True).astype(jnp.float32)  69.3 us
    reduce_scatter x1, waiting for transfers between devices, on_device(): lax.psum_scatter(jnp.where(row_keep[:, None] & col_keep[None, :], sector_...  40.5 us
    all_to_all x1, starting transfers between devices, on_device(): lax.all_to_all(spread, 'sec', split_axis=0, concat_axis=1, tiled=True)[0]  18.8 us
    dot_general x1, matrix products, on_device(): jnp.einsum('ab,akn->bkn', core_cols, lax.all_gather(product, 'mpo', axis=...  17.3 us
    select_n x2, other arithmetic, on_device(): jnp.where(upper_half, jnp.concatenate([partner, mixed], 1), jnp.concatena...  14 us
  transfers between devices with their start and end apart: 5, of which 5 were waited for; matrix products, arithmetic and copies ran while one was open for 0% of the time, Pallas kernels for 0%

commit v1 on v0

--- a/solution.py
+++ b/solution.py
@@ -37,7 +37,9 @@
     mixed = jnp.einsum(
         "ab,akn->bkn",
         core_cols,
-        lax.all_gather(product, "mpo", axis=0, tiled=True).astype(jnp.float32),
+        jnp.concatenate(
+            lax.all_to_all(jnp.stack([product] * lax.axis_size("mpo")), "mpo", 0, 0), axis=0
+        ).astype(jnp.float32),
         precision=lax.Precision.HIGHEST,
     ).astype(jnp.bfloat16)
     for bit_index in range(bit_count):

time: 478 us -> 548 us (1.15)
  waiting for transfers between devices: 375 us -> 435 us
  starting transfers between devices: 27 us -> 33.1 us
  local copies, waits for them, and re-layouts: 16.7 us -> 22.5 us
    all_to_all x0 -> x1, waiting for transfers between devices: none -> 139 us  [on_device(): lax.all_to_all(jnp.stack([product] * lax.axis_size('mpo')), 'mpo', 0, 0)]
    all_gather x1 -> x0, waiting for transfers between devices: 69.3 us -> none  [on_device(): lax.all_gather(product, 'mpo', axis=0, tiled=True).astype(jnp.float32)]
    reduce_scatter x1, waiting for transfers between devices: 40.5 us -> 31.3 us  [on_device(): lax.psum_scatter(jnp.where(row_keep[:, None] & col_keep[None, :], sector_...]
    another operation x0 -> x1, local copies, waits for them, and re-layouts: none -> 6.13 us  [on_device(): jnp.stack([product] * lax.axis_size('mpo'))]
    all_to_all x0 -> x1, starting transfers between devices: none -> 5.49 us  [on_device(): lax.all_to_all(jnp.stack([product] * lax.axis_size('mpo')), 'mpo', 0, 0)]
where the time goes in v1:
time: 548 us
  waiting for transfers between devices  435 us (79%)
  starting transfers between devices  33.1 us (6%)
  matrix products  26.1 us (5%)
  local copies, waits for them, and re-layouts  22.5 us (4%)
  other arithmetic  17.6 us (3%)
  between operations  13.6 us (2%)
    ppermute x2, waiting for transfers between devices, swapped(): lax.ppermute(array, axis, [(i, i ^ 1 << stride) for i in range(lax.axis_s...  168 us
    all_to_all x1, waiting for transfers between devices, on_device(): lax.all_to_all(jnp.stack([product] * lax.axis_size('mpo')), 'mpo', 0, 0)  139 us
    all_to_all x1, waiting for transfers between devices, on_device(): lax.all_to_all(spread, 'sec', split_axis=0, concat_axis=1, tiled=True)[0]  95.8 us
    reduce_scatter x1, waiting for transfers between devices, on_device(): lax.psum_scatter(jnp.where(row_keep[:, None] & col_keep[None, :], sector_...  31.3 us
    all_to_all x1, starting transfers between devices, on_device(): lax.all_to_all(spread, 'sec', split_axis=0, concat_axis=1, tiled=True)[0]  18.8 us
    dot_general x1, matrix products, on_device(): jnp.einsum('ab,akn->bkn', core_cols, jnp.concatenate(lax.all_to_all(jnp.s...  17.3 us
    select_n x2, other arithmetic, on_device(): jnp.where(upper_half, jnp.concatenate([partner, mixed], 1), jnp.concatena...  14 us
  transfers between devices with their start and end apart: 5, of which 5 were waited for; matrix products, arithmetic and copies ran while one was open for 0% of the time, Pallas kernels for 0%

profile of v1, /device:TPU:2, one launch (start us, length us, event | category | flops | bytes accessed | tf_op | source)
XLA Modules:
  0.0 547.9 jit_solution(10558867444505889165)
XLA Ops:
  6.5 0.0 copy-start
  6.5 2.8 broadcast_in_dim.11
  9.3 18.8 %all-to-all-start = ((bf16[64,16,1024]{2,1,0:T(8,128)(2,1)}), bf16[64,16,1024]{2,1,0:T(8,128)(2,1)}, u32[]{:S(2)}, u32[]{:S(2)}) async-start(bf16[64,16,1024]{2,1,0:T(8,128)(2,1)} %bitcast.22), calls=%async_computation | async-start | bytes 4194304 | tf_op jit(solution)/shard_map/all_to_all | solution.py:26
  28.2 0.6 fusion.27
  28.8 0.6 iota_compare_fusion
  29.5 95.8 %all-to-all-done = bf16[64,16,1024]{2,1,0:T(8,128)(2,1)} async-done(((bf16[64,16,1024]{2,1,0:T(8,128)(2,1)}), bf16[64,16,1024]{2,1,0:T(8,128)(2,1)}, u32[]{:S(2)}, u32[]{:S(2)}) %all-to-all-start) | async-done | bytes 2097184 | tf_op jit(solution)/shard_map/all_to_all | solution.py:26
  125.2 3.6 fusion.15
  128.9 0.9 copy.17
  129.8 6.1 %stack.2 = bf16[8,3,256,1024]{3,2,1,0:T(8,128)(2,1)} broadcast(bf16[3,256,1024]{2,1,0:T(8,128)(2,1)S(1)} %copy.17), dimensions={1,2,3} | broadcast | bytes 14155776 | tf_op jit(solution)/shard_map/stack | solution.py:41
  135.9 5.5 %all-to-all-start.1 = ((bf16[8,3,256,1024]{3,2,1,0:T(8,128)(2,1)}), bf16[8,3,256,1024]{3,2,1,0:T(8,128)(2,1)}, u32[]{:S(2)}, u32[]{:S(2)}) async-start(bf16[8,3,256,1024]{3,2,1,0:T(8,128)(2,1)} %stack.2), calls=%async_computation.1 | async-start | bytes 25165824 | tf_op jit(solution)/shard_map/all_to_all | solution.py:41
  141.4 0.0 reduce-scatter.2.cloned.1.call-start
  141.5 139.5 %all-to-all-done.1 = bf16[8,3,256,1024]{3,2,1,0:T(8,128)(2,1)} async-done(((bf16[8,3,256,1024]{3,2,1,0:T(8,128)(2,1)}), bf16[8,3,256,1024]{3,2,1,0:T(8,128)(2,1)}, u32[]{:S(2)}, u32[]{:S(2)}) %all-to-all-start.1) | async-done | bytes 12582944 | tf_op jit(solution)/shard_map/all_to_all | solution.py:41
  280.9 17.3 %fusion.9 = bf16[3,256,1024]{2,0,1:T(4,128)(2,1)S(1)} fusion(bf16[24,256,1024]{2,1,0:T(8,128)(2,1)} %bitcast.5, f32[24,24]{1,0:T(8,128)S(1)} %copy-done.6, s32[]{:T(128)S(6)} %select_n.47), kind=kOutput, calls=%fused_computation.11 | convolution fusion | flops 227278848 | bytes 14158084 | tf_op jit(solution)/shard_map/ab,akn->bkn/dot_general | solution.py:37
  298.2 1.3 copy-done.4
  299.5 0.6 copy.19
  300.1 4.5 collective-permute-start
  304.7 33.9 %collective-permute-done = bf16[3,256,1024]{2,1,0:T(8,128)(2,1)S(1)} collective-permute-done((bf16[3,256,1024]{2,1,0:T(8,128)(2,1)S(1)}, bf16[3,256,1024]{2,1,0:T(8,128)(2,1)S(1)}, u32[]{:S(2)}, u32[]{:S(2)}) %collective-permute-start) | collective-permute-done | bytes 1572896 | tf_op jit(solution)/shard_map/ppermute | solution.py:10
  338.6 1.4 copy.20
  339.9 4.7 maximum_select_fusion.1
  344.6 1.9 copy-done.2
  346.6 2.9 copy.22
  349.5 4.2 collective-permute-start.1
  353.7 0.8 add_compare_fusion
  354.5 134.4 %collective-permute-done.1 = bf16[3,512,1024]{2,1,0:T(8,128)(2,1)} collective-permute-done((bf16[3,512,1024]{2,1,0:T(8,128)(2,1)}, bf16[3,512,1024]{2,1,0:T(8,128)(2,1)}, u32[]{:S(2)}, u32[]{:S(2)}) %collective-permute-start.1) | collective-permute-done | bytes 3145760 | tf_op jit(solution)/shard_map/ppermute | solution.py:10
  489.0 4.6 copy.23
  493.6 0.0 copy-start.7
  493.6 9.3 %maximum_select_fusion = bf16[3,1024,1024]{2,0,1:T(4,128)(2,1)S(1)} fusion(bf16[3,512,1024]{2,0,1:T(4,128)(2,1)S(1)} %copy-done.3, bf16[3,512,1024]{2,0,1:T(4,128)(2,1)S(1)} %copy.23, pred[]{:T(512)S(6)} %eq.16), kind=kLoop, calls=%fused_computation.2 | loop fusion | flops 9437184 | bytes 12582913 | tf_op jit(solution)/shard_map/jit(_where)/select_n | solution.py:48
  502.9 0.0 copy-start.1
  503.0 5.2 fusion.21
  508.2 0.0 reduce-scatter.2.cloned.1.call-update
  508.2 31.3 %reduce-scatter.2.cloned.1.call-done = f32[128,256]{1,0:T(8,128)} async-done(((f32[1024,256]{1,0:T(8,128)}), f32[128,256]{1,0:T(8,128)}) %reduce-scatter.2.cloned.1.call-update) | async-done | bytes 131088 | tf_op jit(solution)/shard_map/reduce_scatter | solution.py:57
  539.5 1.5 convert_element_type.16
  (13 shorter events, 0.0 us)
Async XLA Ops:
  6.5 118.7 %copy-start = (bf16[3,256,1024]{2,1,0:T(8,128)(2,1)S(1)}, bf16[3,256,1024]{2,1,0:T(8,128)(2,1)}, u32[]{:S(2)}) copy-start(bf16[3,256,1024]{2,1,0:T(8,128)(2,1)} %param.6) | copy-start | bytes 4718596
  6.5 21.6 %copy-start.8 = (s32[16]{0:T(128)S(1)}, s32[16]{0:T(128)}, u32[]{:S(2)}) copy-start(s32[16]{0:T(128)} %param.9) | copy-start | bytes 196
  9.3 115.9 %all-to-all-start = ((bf16[64,16,1024]{2,1,0:T(8,128)(2,1)}), bf16[64,16,1024]{2,1,0:T(8,128)(2,1)}, u32[]{:S(2)}, u32[]{:S(2)}) async-start(bf16[64,16,1024]{2,1,0:T(8,128)(2,1)} %bitcast.22), calls=%async_computation | async-start | bytes 4194304 | tf_op jit(solution)/shard_map/all_to_all | solution.py:26
  135.9 145.0 %copy-start.6 = (f32[24,24]{1,0:T(8,128)S(1)}, f32[24,24]{1,0:T(8,128)}, u32[]{:S(2)}) copy-start(f32[24,24]{1,0:T(8,128)} %param.8) | copy-start | bytes 6916
  135.9 145.0 %all-to-all-start.1 = ((bf16[8,3,256,1024]{3,2,1,0:T(8,128)(2,1)}), bf16[8,3,256,1024]{3,2,1,0:T(8,128)(2,1)}, u32[]{:S(2)}, u32[]{:S(2)}) async-start(bf16[8,3,256,1024]{3,2,1,0:T(8,128)(2,1)} %stack.2), calls=%async_computation.1 | async-start | bytes 25165824 | tf_op jit(solution)/shard_map/all_to_all | solution.py:41
  141.4 398.1 %reduce-scatter.2.cloned.1.call-start = ((), (), s32[]{:S(2)}) async-start(), calls=%async_computation.3 | async-start | bytes 1179648 | tf_op jit(solution)/shard_map/reduce_scatter | solution.py:57
  298.2 1.3 copy-start.4
  300.1 38.4 %collective-permute-start = (bf16[3,256,1024]{2,1,0:T(8,128)(2,1)S(1)}, bf16[3,256,1024]{2,1,0:T(8,128)(2,1)S(1)}, u32[]{:S(2)}, u32[]{:S(2)}) collective-permute-start(bf16[3,256,1024]{2,1,0:T(8,128)(2,1)S(1)} %copy.19), channel_id=1, source_target_pairs={{0,1},{1,0},{2,3},{3,2},{4,5},{5,4},{6,7},{7,6},{8,9},{9,8},{10,11... | collective-permute-start | bytes 4718600 | tf_op jit(solution)/shard_map/ppermute | solution.py:10
  304.7 35.3 %copy-start.5 = (bf16[3,256,1024]{2,0,1:T(4,128)(2,1)S(1)}, bf16[3,256,1024]{2,0,1:T(4,128)(2,1)}, u32[]{:S(2)}) copy-start(bf16[3,256,1024]{2,0,1:T(4,128)(2,1)} %copy-done.4) | copy-start | bytes 4718596
  344.6 2.0 copy-start.2
  349.5 139.5 %collective-permute-start.1 = (bf16[3,512,1024]{2,1,0:T(8,128)(2,1)}, bf16[3,512,1024]{2,1,0:T(8,128)(2,1)}, u32[]{:S(2)}, u32[]{:S(2)}) collective-permute-start(bf16[3,512,1024]{2,1,0:T(8,128)(2,1)} %copy.22), channel_id=1, source_target_pairs={{0,2},{1,3},{2,0},{3,1},{4,6},{5,7},{6,4},{7,5},{8,10},{9,11},{10,... | collective-permute-start | bytes 9437192 | tf_op jit(solution)/shard_map/ppermute | solution.py:10
  353.7 139.9 %copy-start.3 = (bf16[3,512,1024]{2,0,1:T(4,128)(2,1)S(1)}, bf16[3,512,1024]{2,0,1:T(4,128)(2,1)}, u32[]{:S(2)}) copy-start(bf16[3,512,1024]{2,0,1:T(4,128)(2,1)} %copy-done.2) | copy-start | bytes 9437188
  493.6 9.3 %copy-start.7 = (bf16[3,256,1024]{2,1,0:T(8,128)(2,1)S(1)}, bf16[3,256,1024]{2,1,0:T(8,128)(2,1)}, u32[]{:S(2)}) copy-start(bf16[3,256,1024]{2,1,0:T(8,128)(2,1)} %param.7) | copy-start | bytes 4718596
  502.9 38.1 %copy-start.1 = (bf16[3,256,1024]{2,1,0:T(8,128)(2,1)S(1)}, bf16[3,256,1024]{2,1,0:T(8,128)(2,1)}, u32[]{:S(2)}) copy-start(bf16[3,256,1024]{2,1,0:T(8,128)(2,1)} %param.6) | copy-start | bytes 4718596
Sparse Core Ops, SparseCore 0:
  508.3 31.1 reduce-scatter.1
